TPU v7x, 512 devices: a whole 4x8x8 slice. The times are simulated.
512 devices in a mesh: ep: 128 (over y, z, core), dp: 4 (over x).
Axes of the slice: x: 4, y: 8, z: 8, core: 2. Of those that a mesh axis runs over, the one named last changes fastest.
Arguments:
- tokens: bfloat16 [2, 2048, 3584], P(None, ('ep', 'dp')), may hold values from -6 to 6
- routing: int32 [2, 2048, 8], P(None, 'ep'), may hold values from 0 to 127, all different within a row; in each aligned block of 16 rows (0 to 15, 16 to 31, ..., all dimensions but the last counted through in order) at most 2 rows name the same one
- gate_values: float32 [2, 2048, 8], P(None, 'ep'), may hold values from 0.05 to 0.5
- held_weight: bfloat16 [128, 3584, 1024], P('ep', None, 'dp'), may hold values from -0.09375 to 0.09375
- scale_table: float32 [128, 28, 8], P(None, None, 'dp'), may hold values from 0.25 to 4
- old_expert: int32 [128], replicated, may hold values from 0 to 127, as said below
- new_expert: int32 [128], replicated, may hold values from 0 to 127, as said below
Outputs:
- combined: bfloat16 [2, 2048, 1024], P(None, 'ep', 'dp')
- moved_weight: bfloat16 [128, 3584, 1024], P('ep', None, 'dp')
Inputs may be any that keep to these rules, and one draw needn't show every extreme that they name: `routing`: each row names 8 different experts; in each aligned block of 16 token rows of a step no expert is named by more than 2 rows. `old_expert`: A permutation of the experts over the slots. `new_expert`: A permutation of the experts over the slots; it equals old_expert except at exactly 32 slots, whose experts are permuted among themselves so that each of them changes.
All inputs are finite; a program needn't handle non-finite values.
Results may differ from a plain program's by a relative error of at most 0.0039.
Values may be sent and summed in bfloat16 or wider, within the bound.
No kernel may reach another device: no remote copies, remote signals or barrier semaphores. Data moves between devices by JAX's collectives and lax.ppermute only.
A program may use at most 64 MiB of HBM per device.

v0:
```python
import jax
import jax.numpy as jnp
from jax import lax
from jax.sharding import PartitionSpec as P


def inverse_place(expert_at):
    count = expert_at.shape[0]
    labels = jnp.arange(count, dtype=jnp.int32)
    match = expert_at[None, :] == labels[:, None]
    return jnp.sum(jnp.where(match, labels[None, :], 0), axis=1)


def source_slots(old_expert, new_expert):
    labels = jnp.arange(old_expert.shape[0], dtype=jnp.int32)
    match = old_expert[None, :] == new_expert[:, None]
    return jnp.sum(jnp.where(match, labels[None, :], 0), axis=1)


def scaled_product(token_rows, weight_block, scales):
    row_blocks = scales.shape[0]
    block_rows = weight_block.shape[0] // row_blocks
    partial_value = jnp.einsum(
        "rbi,bif->rbf",
        token_rows.reshape(token_rows.shape[0], row_blocks, block_rows),
        weight_block.reshape(row_blocks, block_rows, weight_block.shape[1]),
        preferred_element_type=jnp.float32,
    )
    widened = jnp.repeat(scales, weight_block.shape[1] // scales.shape[1], axis=1)
    return jnp.sum(partial_value * widened[None, :, :], axis=1)


def expert_service(weight_block, scales):

    def serve_rows(arrived):

        def one_slot(slot_rows):
            return jax.nn.silu(scaled_product(slot_rows, weight_block, scales)).astype(jnp.bfloat16)

        activated = lax.map(one_slot, arrived)
        return lax.all_to_all(activated, "ep", split_axis=1, concat_axis=1, tiled=True)

    return serve_rows


def route_pairs(routing, expert_at, peers):
    pair_ids = routing.reshape(-1)
    labels = jnp.arange(peers, dtype=jnp.int32)
    onehot = (pair_ids[:, None] == labels[None, :]).astype(jnp.int32)
    before = jnp.cumsum(onehot, axis=0) - onehot
    slot_rank = jnp.sum(before * onehot, axis=1)
    owners = jnp.sum(onehot * inverse_place(expert_at)[None, :], axis=1)
    return slot_rank * peers + owners


def shards(tokens, routing, gate_values, held_weight, scale_table, old_expert, new_expert):
    peers = lax.axis_size("ep")
    my_slot = lax.axis_index("ep")
    group_size = routing.shape[1]
    top_count = routing.shape[2]
    capacity = min(group_size, max(2, 2 * group_size * top_count // peers))
    hidden_width = held_weight.shape[2]
    old_block = held_weight[0]
    sources = source_slots(old_expert, new_expert)
    pieces = old_block.reshape(peers, old_block.shape[0] // peers, hidden_width)
    new_block = lax.all_to_all(
        jnp.take(
            lax.all_to_all(pieces, "ep", split_axis=0, concat_axis=0, tiled=True), sources, axis=0
        ),
        "ep",
        split_axis=0,
        concat_axis=0,
        tiled=True,
    ).reshape(old_block.shape)
    first_serve = (new_block, new_expert)
    serve_plans = [first_serve] + [(new_block, new_expert)] * (tokens.shape[0] - 1)
    grouped = lax.all_gather(tokens, "dp", axis=1, tiled=True)
    columns = grouped.shape[2]
    combined_steps = []
    for decode_step in range(tokens.shape[0]):
        weight_block, expert_at = serve_plans[decode_step]
        scales = scale_table[expert_at[my_slot]]
        target = route_pairs(routing[decode_step], expert_at, peers)
        repeated = jnp.repeat(grouped[decode_step], top_count, axis=0)
        send_buffer = jnp.zeros((capacity * peers, columns), grouped.dtype).at[target].set(repeated)
        send_buffer = send_buffer.reshape(capacity, peers, columns)
        serve_rows = expert_service(weight_block, scales)
        returned = serve_rows(
            lax.all_to_all(send_buffer, "ep", split_axis=1, concat_axis=1, tiled=True)
        )
        activated = returned.reshape(capacity * peers, hidden_width)[target].astype(jnp.float32)
        activated = activated.reshape(group_size, top_count, hidden_width)
        weighted = jnp.sum(gate_values[decode_step][:, :, None] * activated, axis=1)
        combined_steps.append(weighted.astype(jnp.bfloat16))
    return (jnp.stack(combined_steps), new_block[None])


def solution(mesh):
    placed = (
        P(None, ("ep", "dp"), None),
        P(None, "ep", None),
        P(None, "ep", None),
        P("ep", None, "dp"),
        P(None, None, "dp"),
        P(),
        P(),
    )
    return jax.shard_map(
        shards,
        mesh=mesh,
        in_specs=placed,
        out_specs=(P(None, "ep", "dp"), P("ep", None, "dp")),
        check_vma=False,
    )
```

profile of v0, /device:TPU:1, one launch (start us, length us, event | category | flops | bytes accessed | tf_op | source)
XLA Modules:
  0.0 315.5 jit_solution(4355905081281846887)
XLA Ops:
  3.1 10.5 %all_gather.3 = bf16[2,16,3584]{2,0,1:T(2,128)(2,1)S(1)} all-gather(bf16[2,4,3584]{2,0,1:T(2,128)(2,1)S(1)} %copy.58), channel_id=1, replica_groups=mesh['ep'=128,'dp'=4] {'dp'}, dimensions={1}, use_global_device_ids=true | all-gather | bytes 286720 | tf_op jit(solution)/shard_map/all_gather | solution.py:77
  15.1 2.5 scatter_custom_fusion
  17.5 3.1 copy.60
  20.7 20.5 %all-to-all-start = ((bf16[2,128,3584]{2,0,1:T(2,128)(2,1)}), bf16[2,128,3584]{2,0,1:T(2,128)(2,1)S(1)}, u32[]{:S(2)}, u32[]{:S(2)}) async-start(bf16[2,128,3584]{2,0,1:T(2,128)(2,1)} %copy.60), calls=%async_computation | async-start | bytes 3670016 | tf_op jit(solution)/shard_map/all_to_all | solution.py:89
  41.1 3.7 %reshape_squeeze.3 = bf16[128,28,256]{2,1,0:T(8,128)(2,1)} reshape(bf16[1,3584,256]{2,1,0:T(8,128)(2,1)} %param.14) | data formatting | bytes 3670016 | tf_op jit(solution)/shard_map/reshape;squeeze | solution.py:65
  44.9 42.7 %all-to-all-done = bf16[2,128,3584]{2,0,1:T(2,128)(2,1)S(1)} async-done(((bf16[2,128,3584]{2,0,1:T(2,128)(2,1)}), bf16[2,128,3584]{2,0,1:T(2,128)(2,1)S(1)}, u32[]{:S(2)}, u32[]{:S(2)}) %all-to-all-start) | async-done | bytes 1835040 | tf_op jit(solution)/shard_map/all_to_all | solution.py:89
  87.6 1.3 copy-done.3
  88.9 7.8 %all-to-all-start.1 = ((bf16[128,28,256]{2,1,0:T(8,128)(2,1)}), bf16[128,28,256]{2,1,0:T(8,128)(2,1)S(1)}, u32[]{:S(2)}, u32[]{:S(2)}) async-start(bf16[128,28,256]{2,1,0:T(8,128)(2,1)} %reshape_squeeze.3), calls=%async_computation.1 | async-start | bytes 4194304 | tf_op jit(solution)/shard_map/all_to_all | solution.py:68
  96.7 3.3 %scatter_custom_fusion.1 = bf16[256,3584]{1,0:T(8,128)(2,1)} fusion(s32[128]{0:T(128)S(1)} %get-tuple-element.141, bf16[]{:T(256)} %constant.58.clone.1, bf16[16,3584]{1,0:T(8,128)(2,1)S(1)} %get-tuple-element.142), kind=kCustom, calls=%fused_computation.24 | custom fusion | bytes 1949698 | tf_op jit(solution)/shard_map/scatter | solution.py:85
  100.0 4.6 %copy.69 = bf16[2,128,3584]{2,0,1:T(2,128)(2,1)} copy(bf16[2,128,3584]{2,1,0:T(8,128)(2,1)} %bitcast.125) | data formatting | bytes 3670016 | tf_op jit(solution)/shard_map/reshape | solution.py:86
  104.6 44.2 %all-to-all-done.1 = bf16[128,28,256]{2,1,0:T(8,128)(2,1)S(1)} async-done(((bf16[128,28,256]{2,1,0:T(8,128)(2,1)}), bf16[128,28,256]{2,1,0:T(8,128)(2,1)S(1)}, u32[]{:S(2)}, u32[]{:S(2)}) %all-to-all-start.1) | async-done | bytes 1835040 | tf_op jit(solution)/shard_map/all_to_all | solution.py:68
  148.8 8.1 %all-to-all-start.4 = ((bf16[2,128,3584]{2,0,1:T(2,128)(2,1)}), bf16[2,128,3584]{2,0,1:T(2,128)(2,1)}, u32[]{:S(2)}, u32[]{:S(2)}) async-start(bf16[2,128,3584]{2,0,1:T(2,128)(2,1)} %copy.69), calls=%async_computation.4 | async-start | bytes 3670016 | tf_op jit(solution)/shard_map/all_to_all | solution.py:89
  157.0 2.0 gather_fusion
  159.0 3.2 %broadcast_select_fusion = bf16[128,28,256]{2,1,0:T(8,128)(2,1)} fusion(bf16[128,28,256]{2,1,0:T(8,128)(2,1)} %gather_fusion, pred[128]{0:T(512)(128)(4,1)S(1)} %compare_and_fusion), kind=kLoop, calls=%fused_computation.23 | loop fusion | flops 917504 | bytes 3670144 | tf_op jit(solution)/shard_map/jit(_take)/select_n | solution.py:67
  162.2 40.9 %all-to-all-done.4 = bf16[2,128,3584]{2,0,1:T(2,128)(2,1)} async-done(((bf16[2,128,3584]{2,0,1:T(2,128)(2,1)}), bf16[2,128,3584]{2,0,1:T(2,128)(2,1)}, u32[]{:S(2)}, u32[]{:S(2)}) %all-to-all-start.4) | async-done | bytes 1835040 | tf_op jit(solution)/shard_map/all_to_all | solution.py:89
  203.1 7.8 %all-to-all-start.2 = ((bf16[128,28,256]{2,1,0:T(8,128)(2,1)}), bf16[128,28,256]{2,1,0:T(8,128)(2,1)S(1)}, u32[]{:S(2)}, u32[]{:S(2)}) async-start(bf16[128,28,256]{2,1,0:T(8,128)(2,1)} %broadcast_select_fusion), calls=%async_computation.2 | async-start | bytes 4194304 | tf_op jit(solution)/shard_map/all_to_all | solution.py:66
  213.8 5.6 %copy.62 = bf16[2,128,3584]{1,2,0:T(8,128)(2,1)} copy(bf16[2,128,3584]{2,0,1:T(2,128)(2,1)} %copy-done.3) | data formatting | bytes 3670016 | tf_op jit(solution)/shard_map/while | solution.py:40
  219.3 5.5 %copy.70 = bf16[2,128,3584]{1,2,0:T(8,128)(2,1)} copy(bf16[2,128,3584]{2,0,1:T(2,128)(2,1)} %all-to-all-done.4) | data formatting | bytes 3670016 | tf_op jit(solution)/shard_map/while | solution.py:40
  224.9 38.2 %all-to-all-done.2 = bf16[128,28,256]{2,1,0:T(8,128)(2,1)S(1)} async-done(((bf16[128,28,256]{2,1,0:T(8,128)(2,1)}), bf16[128,28,256]{2,1,0:T(8,128)(2,1)S(1)}, u32[]{:S(2)}, u32[]{:S(2)}) %all-to-all-start.2) | async-done | bytes 1835040 | tf_op jit(solution)/shard_map/all_to_all | solution.py:66
  263.1 1.5 reshape_reshape.6
  265.0 5.2 %while.22 = (s32[]{:T(128)}, bf16[2,128,256]{2,1,0:T(8,128)(2,1)S(1)}, bf16[2,128,3584]{1,2,0:T(8,128)(2,1)}, bf16[128,28,256]{2,1,0:T(8,128)(2,1)}, f32[28,2]{1...) while((s32[]{:T(128)}, bf16[2,128,256]{2,1,0:T(8,128)(2,1)S(1)}, ...), condition=%wide.wide.region_8.9_spmd, body=%wide.wide.region_6.8_spmd.sunk | while | flops 236847104 | bytes 12439901 | solution.py:40
  265.0 1.4 constant_dynamic-slice_fusion.7
  267.6 1.4 constant_dynamic-slice_fusion.7
  270.9 7.7 %all-to-all-start.3 = ((bf16[2,128,256]{2,0,1:T(2,128)(2,1)}), bf16[2,128,256]{2,0,1:T(2,128)(2,1)S(1)}, u32[]{:S(2)}, u32[]{:S(2)}) async-start(bf16[2,128,256]{2,0,1:T(2,128)(2,1)} %copy.64), calls=%async_computation.3 | async-start | bytes 262144 | tf_op jit(solution)/shard_map/all_to_all | solution.py:41
  278.7 3.9 %reshape_reshape.8 = bf16[28,128,256]{2,1,0:T(8,128)(2,1)} reshape(bf16[128,28,256]{2,1,0:T(8,128)(2,1)} %get-tuple-element.307) | data formatting | bytes 3670016 | tf_op jit(solution)/shard_map/while/body/eval_jaxpr/reshape;reshape | solution.py:26
  282.6 4.6 %while.23 = (s32[]{:T(128)}, bf16[2,128,256]{2,1,0:T(8,128)(2,1)S(1)}, bf16[2,128,3584]{1,2,0:T(8,128)(2,1)S(1)}, bf16[128,28,256]{2,1,0:T(8,128)(2,1)}, f32[28,...) while((s32[]{:T(128)}, bf16[2,128,256]{2,1,0:T(8,128)(2,1)S(1)}, ...), condition=%wide.wide.region_16.17_spmd, body=%wide.wide.region_14.16_spmd.sunk | while | flops 236847104 | bytes 12439901 | solution.py:40
  282.8 1.3 copy-done.4
  285.1 1.3 copy-done.4
  288.0 3.0 all-to-all-done.3
  290.9 10.8 %all-to-all-start.5 = ((bf16[2,128,256]{2,0,1:T(2,128)(2,1)}), bf16[2,128,256]{2,0,1:T(2,128)(2,1)S(1)}, u32[]{:S(2)}, u32[]{:S(2)}) async-start(bf16[2,128,256]{2,0,1:T(2,128)(2,1)} %copy.72), calls=%async_computation.5 | async-start | bytes 262144 | tf_op jit(solution)/shard_map/all_to_all | solution.py:41
  301.9 3.7 %broadcast_in_dim_reshape.3 = bf16[1,3584,256]{2,1,0:T(8,128)(2,1)} reshape(bf16[128,28,256]{2,1,0:T(8,128)(2,1)} %get-tuple-element.308) | data formatting | bytes 3670016 | tf_op jit(solution)/shard_map/broadcast_in_dim;reshape | solution.py:95
  306.6 7.3 %all-to-all-done.5 = bf16[2,128,256]{2,0,1:T(2,128)(2,1)S(1)} async-done(((bf16[2,128,256]{2,0,1:T(2,128)(2,1)}), bf16[2,128,256]{2,0,1:T(2,128)(2,1)S(1)}, u32[]{:S(2)}, u32[]{:S(2)}) %all-to-all-start.5) | async-done | bytes 131104 | tf_op jit(solution)/shard_map/all_to_all | solution.py:41
  (77 shorter events, 13.6 us)
Async XLA Ops:
  0.6 212.8 %copy-start = (f32[128,28,2]{0,2,1:T(2,128)S(1)}, f32[128,28,2]{0,2,1:T(2,128)}, u32[]{:S(2)}) copy-start(f32[128,28,2]{0,2,1:T(2,128)} %param.15) | copy-start | bytes 86020
  20.7 67.0 %all-to-all-start = ((bf16[2,128,3584]{2,0,1:T(2,128)(2,1)}), bf16[2,128,3584]{2,0,1:T(2,128)(2,1)S(1)}, u32[]{:S(2)}, u32[]{:S(2)}) async-start(bf16[2,128,3584]{2,0,1:T(2,128)(2,1)} %copy.60), calls=%async_computation | async-start | bytes 3670016 | tf_op jit(solution)/shard_map/all_to_all | solution.py:89
  87.6 1.3 copy-start.3
  88.9 59.9 %all-to-all-start.1 = ((bf16[128,28,256]{2,1,0:T(8,128)(2,1)}), bf16[128,28,256]{2,1,0:T(8,128)(2,1)S(1)}, u32[]{:S(2)}, u32[]{:S(2)}) async-start(bf16[128,28,256]{2,1,0:T(8,128)(2,1)} %reshape_squeeze.3), calls=%async_computation.1 | async-start | bytes 4194304 | tf_op jit(solution)/shard_map/all_to_all | solution.py:68
  148.8 54.3 %all-to-all-start.4 = ((bf16[2,128,3584]{2,0,1:T(2,128)(2,1)}), bf16[2,128,3584]{2,0,1:T(2,128)(2,1)}, u32[]{:S(2)}, u32[]{:S(2)}) async-start(bf16[2,128,3584]{2,0,1:T(2,128)(2,1)} %copy.69), calls=%async_computation.4 | async-start | bytes 3670016 | tf_op jit(solution)/shard_map/all_to_all | solution.py:89
  162.2 48.7 %copy-start.7 = (s32[128]{0:T(128)S(1)}, s32[128]{0:T(128)}, u32[]{:S(2)}) copy-start(s32[128]{0:T(128)} %param.17) | copy-start | bytes 1540
  162.2 51.5 %copy-start.6 = (f32[2,16,8]{1,2,0:T(8,128)S(1)}, f32[2,16,8]{1,2,0:T(8,128)}, u32[]{:S(2)}) copy-start(f32[2,16,8]{1,2,0:T(8,128)} %param.13) | copy-start | bytes 3076
  203.1 59.9 %all-to-all-start.2 = ((bf16[128,28,256]{2,1,0:T(8,128)(2,1)}), bf16[128,28,256]{2,1,0:T(8,128)(2,1)S(1)}, u32[]{:S(2)}, u32[]{:S(2)}) async-start(bf16[128,28,256]{2,1,0:T(8,128)(2,1)} %broadcast_select_fusion), calls=%async_computation.2 | async-start | bytes 4194304 | tf_op jit(solution)/shard_map/all_to_all | solution.py:66
  263.1 1.9 copy-start.1
  265.0 1.8 copy-start.5
  267.6 1.8 copy-start.5
  270.9 20.0 %all-to-all-start.3 = ((bf16[2,128,256]{2,0,1:T(2,128)(2,1)}), bf16[2,128,256]{2,0,1:T(2,128)(2,1)S(1)}, u32[]{:S(2)}, u32[]{:S(2)}) async-start(bf16[2,128,256]{2,0,1:T(2,128)(2,1)} %copy.64), calls=%async_computation.3 | async-start | bytes 262144 | tf_op jit(solution)/shard_map/all_to_all | solution.py:41
  278.7 3.9 %copy-start.2 = (bf16[2,128,3584]{1,2,0:T(8,128)(2,1)S(1)}, bf16[2,128,3584]{1,2,0:T(8,128)(2,1)}, u32[]{:S(2)}) copy-start(bf16[2,128,3584]{1,2,0:T(8,128)(2,1)} %copy.70) | copy-start | bytes 5505028
  282.6 1.5 copy-start.4
  284.9 1.5 copy-start.4
  290.9 22.9 %all-to-all-start.5 = ((bf16[2,128,256]{2,0,1:T(2,128)(2,1)}), bf16[2,128,256]{2,0,1:T(2,128)(2,1)S(1)}, u32[]{:S(2)}, u32[]{:S(2)}) async-start(bf16[2,128,256]{2,0,1:T(2,128)(2,1)} %copy.72), calls=%async_computation.5 | async-start | bytes 262144 | tf_op jit(solution)/shard_map/all_to_all | solution.py:41
where the time goes:
time: 317 us; the launch traced here: 315 us
  waiting for transfers between devices  176 us (56%)
  starting transfers between devices  62.7 us (20%)
  local copies, waits for them, and re-layouts  54.2 us (17%)
  blocking collectives  10.5 us (3%)
  other arithmetic  5.92 us (2%)
    all_to_all x2, waiting for transfers between devices, shards(): lax.all_to_all(send_buffer, 'ep', split_axis=1, concat_axis=1, tiled=True)  83.6 us
    all_to_all x1, waiting for transfers between devices, shards(): lax.all_to_all(pieces, 'ep', split_axis=0, concat_axis=0, tiled=True)  44.2 us
    all_to_all x1, waiting for transfers between devices, shards(): lax.all_to_all(jnp.take(lax.all_to_all(pieces, 'ep', split_axis=0, concat...  38.2 us
    all_to_all x2, starting transfers between devices, shards(): lax.all_to_all(send_buffer, 'ep', split_axis=1, concat_axis=1, tiled=True)  28.6 us
    all_to_all x2, starting transfers between devices, serve_rows(): lax.all_to_all(activated, 'ep', split_axis=1, concat_axis=1, tiled=True)  18.5 us
    while x5, local copies, waits for them, and re-layouts, serve_rows(): activated = lax.map(one_slot, arrived)  12.7 us
    all_gather x1, blocking collectives, shards(): grouped = lax.all_gather(tokens, 'dp', axis=1, tiled=True)  10.5 us
    all_to_all x2, waiting for transfers between devices, serve_rows(): lax.all_to_all(activated, 'ep', split_axis=1, concat_axis=1, tiled=True)  10.3 us
  transfers between devices with their start and end apart: 6, of which 6 were waited for; matrix products, arithmetic and copies ran while one was open for 13% of the time, Pallas kernels for 0%

commit v1 on v0

--- a/solution.py
+++ b/solution.py
@@ -2,6 +2,13 @@
 import jax.numpy as jnp
 from jax import lax
 from jax.sharding import PartitionSpec as P
+
+
+def trade_parts(x, name, split, join):
+    peers = lax.axis_size(name)
+    blocks = jnp.stack(jnp.split(x, peers, axis=split), axis=0)
+    blocks = lax.all_to_all(blocks, name, split_axis=0, concat_axis=0)
+    return jnp.concatenate(blocks, axis=join)
 
 
 def inverse_place(expert_at):
@@ -38,7 +45,7 @@
             return jax.nn.silu(scaled_product(slot_rows, weight_block, scales)).astype(jnp.bfloat16)
 
         activated = lax.map(one_slot, arrived)
-        return lax.all_to_all(activated, "ep", split_axis=1, concat_axis=1, tiled=True)
+        return trade_parts(activated, "ep", 1, 1)
 
     return serve_rows
 

time: 317 us -> 463 us (1.46)
  local copies, waits for them, and re-layouts: 54.2 us -> 199 us
    unnamed x13 -> x267, local copies, waits for them, and re-layouts: 2.49 us -> 147 us
  transfers between devices with their start and end apart: 6 -> 6, of which waited for: 6 -> 5; matrix products, arithmetic and copies ran while one was open for 13% -> 24% of each run, Pallas kernels for 0% -> 0%
where the time goes in v1:
time: 463 us; the launch traced here: 461 us
  local copies, waits for them, and re-layouts  199 us (43%)
  waiting for transfers between devices  174 us (38%)
  starting transfers between devices  65.6 us (14%)
  blocking collectives  10.5 us (2%)
  other arithmetic  5.92 us (1%)
    unnamed x267, local copies, waits for them, and re-layouts  147 us
    all_to_all x2, waiting for transfers between devices, shards(): lax.all_to_all(send_buffer, 'ep', split_axis=1, concat_axis=1, tiled=True)  83.6 us
    all_to_all x1, waiting for transfers between devices, shards(): lax.all_to_all(pieces, 'ep', split_axis=0, concat_axis=0, tiled=True)  44.2 us
    all_to_all x1, waiting for transfers between devices, shards(): lax.all_to_all(jnp.take(lax.all_to_all(pieces, 'ep', split_axis=0, concat...  38.2 us
    all_to_all x2, starting transfers between devices, shards(): lax.all_to_all(send_buffer, 'ep', split_axis=1, concat_axis=1, tiled=True)  28.6 us
    all_to_all x2, starting transfers between devices, trade_parts(): blocks = lax.all_to_all(blocks, name, split_axis=0, concat_axis=0)  21.5 us
    while x5, local copies, waits for them, and re-layouts, serve_rows(): activated = lax.map(one_slot, arrived)  11.5 us
    all_gather x1, blocking collectives, shards(): grouped = lax.all_gather(tokens, 'dp', axis=1, tiled=True)  10.5 us
  transfers between devices with their start and end apart: 6, of which 5 were waited for; matrix products, arithmetic and copies ran while one was open for 24% of the time, Pallas kernels for 0%

profile of v1, /device:TPU:1, one launch (start us, length us, event | category | flops | bytes accessed | tf_op | source)
XLA Modules:
  0.0 461.4 jit_solution(8139449419542059061)
XLA Ops:
  3.1 10.5 %all_gather.3 = bf16[2,16,3584]{2,0,1:T(2,128)(2,1)S(1)} all-gather(bf16[2,4,3584]{2,0,1:T(2,128)(2,1)S(1)} %copy.1078), channel_id=1, replica_groups=mesh['ep'=128,'dp'=4] {'dp'}, dimensions={1}, use_global_device_ids=true | all-gather | bytes 286720 | tf_op jit(solution)/shard_map/all_gather | solution.py:84
  13.9 0.9 select_reduce_fusion.2
  15.1 2.5 scatter_custom_fusion
  17.5 3.1 copy.1080
  20.7 20.5 %all-to-all-start = ((bf16[2,128,3584]{2,0,1:T(2,128)(2,1)}), bf16[2,128,3584]{2,0,1:T(2,128)(2,1)S(1)}, u32[]{:S(2)}, u32[]{:S(2)}) async-start(bf16[2,128,3584]{2,0,1:T(2,128)(2,1)} %copy.1080), calls=%async_computation | async-start | bytes 3670016 | tf_op jit(solution)/shard_map/all_to_all | solution.py:96
  41.1 3.7 reshape_squeeze.3
  44.9 42.7 %all-to-all-done = bf16[2,128,3584]{2,0,1:T(2,128)(2,1)S(1)} async-done(((bf16[2,128,3584]{2,0,1:T(2,128)(2,1)}), bf16[2,128,3584]{2,0,1:T(2,128)(2,1)S(1)}, u32[]{:S(2)}, u32[]{:S(2)}) %all-to-all-start) | async-done | bytes 1835040 | tf_op jit(solution)/shard_map/all_to_all | solution.py:96
  87.6 1.3 copy-done.3
  88.9 7.8 %all-to-all-start.1 = ((bf16[128,28,256]{2,1,0:T(8,128)(2,1)}), bf16[128,28,256]{2,1,0:T(8,128)(2,1)S(1)}, u32[]{:S(2)}, u32[]{:S(2)}) async-start(bf16[128,28,256]{2,1,0:T(8,128)(2,1)} %reshape_squeeze.3), calls=%async_computation.1 | async-start | bytes 4194304 | tf_op jit(solution)/shard_map/all_to_all | solution.py:75
  96.7 3.3 scatter_custom_fusion.1
  100.0 4.6 %copy.1215 = bf16[2,128,3584]{2,0,1:T(2,128)(2,1)} copy(bf16[2,128,3584]{2,1,0:T(8,128)(2,1)} %bitcast.1147) | data formatting | bytes 3670016 | tf_op jit(solution)/shard_map/reshape | solution.py:93
  104.6 44.2 %all-to-all-done.1 = bf16[128,28,256]{2,1,0:T(8,128)(2,1)S(1)} async-done(((bf16[128,28,256]{2,1,0:T(8,128)(2,1)}), bf16[128,28,256]{2,1,0:T(8,128)(2,1)S(1)}, u32[]{:S(2)}, u32[]{:S(2)}) %all-to-all-start.1) | async-done | bytes 1835040 | tf_op jit(solution)/shard_map/all_to_all | solution.py:75
  148.8 8.1 %all-to-all-start.4 = ((bf16[2,128,3584]{2,0,1:T(2,128)(2,1)}), bf16[2,128,3584]{2,0,1:T(2,128)(2,1)}, u32[]{:S(2)}, u32[]{:S(2)}) async-start(bf16[2,128,3584]{2,0,1:T(2,128)(2,1)} %copy.1215), calls=%async_computation.4 | async-start | bytes 3670016 | tf_op jit(solution)/shard_map/all_to_all | solution.py:96
  157.0 2.0 gather_fusion
  159.0 3.2 broadcast_select_fusion
  162.2 40.9 %all-to-all-done.4 = bf16[2,128,3584]{2,0,1:T(2,128)(2,1)} async-done(((bf16[2,128,3584]{2,0,1:T(2,128)(2,1)}), bf16[2,128,3584]{2,0,1:T(2,128)(2,1)}, u32[]{:S(2)}, u32[]{:S(2)}) %all-to-all-start.4) | async-done | bytes 1835040 | tf_op jit(solution)/shard_map/all_to_all | solution.py:96
  203.1 7.8 %all-to-all-start.2 = ((bf16[128,28,256]{2,1,0:T(8,128)(2,1)}), bf16[128,28,256]{2,1,0:T(8,128)(2,1)S(1)}, u32[]{:S(2)}, u32[]{:S(2)}) async-start(bf16[128,28,256]{2,1,0:T(8,128)(2,1)} %broadcast_select_fusion), calls=%async_computation.2 | async-start | bytes 4194304 | tf_op jit(solution)/shard_map/all_to_all | solution.py:73
  213.8 5.5 %copy.1082 = bf16[2,128,3584]{1,2,0:T(8,128)(2,1)} copy(bf16[2,128,3584]{2,0,1:T(2,128)(2,1)} %copy-done.3) | data formatting | bytes 3670016 | tf_op jit(solution)/shard_map/while | solution.py:47
  219.3 5.5 %copy.1216 = bf16[2,128,3584]{1,2,0:T(8,128)(2,1)} copy(bf16[2,128,3584]{2,0,1:T(2,128)(2,1)} %all-to-all-done.4) | data formatting | bytes 3670016 | tf_op jit(solution)/shard_map/while | solution.py:47
  224.9 38.2 %all-to-all-done.2 = bf16[128,28,256]{2,1,0:T(8,128)(2,1)S(1)} async-done(((bf16[128,28,256]{2,1,0:T(8,128)(2,1)}), bf16[128,28,256]{2,1,0:T(8,128)(2,1)S(1)}, u32[]{:S(2)}, u32[]{:S(2)}) %all-to-all-start.2) | async-done | bytes 1835040 | tf_op jit(solution)/shard_map/all_to_all | solution.py:73
  263.1 1.5 reshape_reshape.14
  265.0 5.2 %while.22 = (s32[]{:T(128)}, bf16[2,128,256]{2,1,0:T(8,128)(2,1)S(1)}, bf16[2,128,3584]{1,2,0:T(8,128)(2,1)}, bf16[128,28,256]{2,1,0:T(8,128)(2,1)}, f32[28,2]{1...) while((s32[]{:T(128)}, bf16[2,128,256]{2,1,0:T(8,128)(2,1)S(1)}, ...), condition=%wide.wide.region_8.9_spmd, body=%wide.wide.region_6.8_spmd.sunk | while | flops 236847104 | bytes 12439901 | solution.py:47
  265.0 1.4 constant_dynamic-slice_fusion.7
  267.6 1.4 constant_dynamic-slice_fusion.7
  343.2 7.7 %all-to-all-start.3 = ((bf16[128,2,1,256]{3,1,2,0:T(2,128)(2,1)}), bf16[128,2,1,256]{3,1,2,0:T(2,128)(2,1)S(1)}, u32[]{:S(2)}, u32[]{:S(2)}) async-start(bf16[128,2,1,256]{3,1,2,0:T(2,128)(2,1)} %constant_dynamic-update-slice_fusion), calls=%async_computation.3 | async-start | bytes 262144 | tf_op jit(solution)/shard_map/all_to_all | solution.py:10
  350.9 3.9 reshape_reshape.16
  354.8 4.6 while.23
  355.0 1.3 copy-done.4
  357.3 1.3 copy-done.4
  432.9 13.7 %all-to-all-start.5 = ((bf16[128,2,1,256]{3,1,2,0:T(2,128)(2,1)}), bf16[128,2,1,256]{3,1,2,0:T(2,128)(2,1)S(1)}, u32[]{:S(2)}, u32[]{:S(2)}) async-start(bf16[128,2,1,256]{3,1,2,0:T(2,128)(2,1)} %constant_dynamic-update-slice_fusion.128), calls=%async_computation.5 | async-start | bytes 262144 | tf_op jit(solution)/shard_map/all_to_all | solution.py:10
  446.8 3.7 broadcast_in_dim_reshape.3
  450.6 8.2 %all-to-all-done.5 = bf16[128,2,1,256]{3,1,2,0:T(2,128)(2,1)S(1)} async-done(((bf16[128,2,1,256]{3,1,2,0:T(2,128)(2,1)}), bf16[128,2,1,256]{3,1,2,0:T(2,128)(2,1)S(1)}, u32[]{:S(2)}, u32[]{:S(2)}) %all-to-all-start.5) | async-done | bytes 131104 | tf_op jit(solution)/shard_map/all_to_all | solution.py:10
  (335 shorter events, 157.5 us)
Async XLA Ops:
  0.6 212.8 %copy-start = (f32[128,28,2]{0,2,1:T(2,128)S(1)}, f32[128,28,2]{0,2,1:T(2,128)}, u32[]{:S(2)}) copy-start(f32[128,28,2]{0,2,1:T(2,128)} %param.15) | copy-start | bytes 86020
  20.7 67.0 %all-to-all-start = ((bf16[2,128,3584]{2,0,1:T(2,128)(2,1)}), bf16[2,128,3584]{2,0,1:T(2,128)(2,1)S(1)}, u32[]{:S(2)}, u32[]{:S(2)}) async-start(bf16[2,128,3584]{2,0,1:T(2,128)(2,1)} %copy.1080), calls=%async_computation | async-start | bytes 3670016 | tf_op jit(solution)/shard_map/all_to_all | solution.py:96
  87.6 1.3 copy-start.3
  88.9 59.9 %all-to-all-start.1 = ((bf16[128,28,256]{2,1,0:T(8,128)(2,1)}), bf16[128,28,256]{2,1,0:T(8,128)(2,1)S(1)}, u32[]{:S(2)}, u32[]{:S(2)}) async-start(bf16[128,28,256]{2,1,0:T(8,128)(2,1)} %reshape_squeeze.3), calls=%async_computation.1 | async-start | bytes 4194304 | tf_op jit(solution)/shard_map/all_to_all | solution.py:75
  148.8 54.3 %all-to-all-start.4 = ((bf16[2,128,3584]{2,0,1:T(2,128)(2,1)}), bf16[2,128,3584]{2,0,1:T(2,128)(2,1)}, u32[]{:S(2)}, u32[]{:S(2)}) async-start(bf16[2,128,3584]{2,0,1:T(2,128)(2,1)} %copy.1215), calls=%async_computation.4 | async-start | bytes 3670016 | tf_op jit(solution)/shard_map/all_to_all | solution.py:96
  162.2 48.7 %copy-start.7 = (s32[128]{0:T(128)S(1)}, s32[128]{0:T(128)}, u32[]{:S(2)}) copy-start(s32[128]{0:T(128)} %param.17) | copy-start | bytes 1540
  203.1 59.9 %all-to-all-start.2 = ((bf16[128,28,256]{2,1,0:T(8,128)(2,1)}), bf16[128,28,256]{2,1,0:T(8,128)(2,1)S(1)}, u32[]{:S(2)}, u32[]{:S(2)}) async-start(bf16[128,28,256]{2,1,0:T(8,128)(2,1)} %broadcast_select_fusion), calls=%async_computation.2 | async-start | bytes 4194304 | tf_op jit(solution)/shard_map/all_to_all | solution.py:73
  263.1 1.9 copy-start.1
  265.0 1.8 copy-start.5
  267.6 1.8 copy-start.5
  343.2 89.7 %all-to-all-start.3 = ((bf16[128,2,1,256]{3,1,2,0:T(2,128)(2,1)}), bf16[128,2,1,256]{3,1,2,0:T(2,128)(2,1)S(1)}, u32[]{:S(2)}, u32[]{:S(2)}) async-start(bf16[128,2,1,256]{3,1,2,0:T(2,128)(2,1)} %constant_dynamic-update-slice_fusion), calls=%async_computation.3 | async-start | bytes 262144 | tf_op jit(solution)/shard_map/all_to_all | solution.py:10
  350.9 3.9 copy-start.2
  354.8 91.8 %copy-start.6 = (f32[2,16,8]{1,2,0:T(8,128)S(1)}, f32[2,16,8]{1,2,0:T(8,128)}, u32[]{:S(2)}) copy-start(f32[2,16,8]{1,2,0:T(8,128)} %param.13) | copy-start | bytes 3076
  354.8 1.5 copy-start.4
  357.1 1.5 copy-start.4
  432.9 25.9 %all-to-all-start.5 = ((bf16[128,2,1,256]{3,1,2,0:T(2,128)(2,1)}), bf16[128,2,1,256]{3,1,2,0:T(2,128)(2,1)S(1)}, u32[]{:S(2)}, u32[]{:S(2)}) async-start(bf16[128,2,1,256]{3,1,2,0:T(2,128)(2,1)} %constant_dynamic-update-slice_fusion.128), calls=%async_computation.5 | async-start | bytes 262144 | tf_op jit(solution)/shard_map/all_to_all | solution.py:10
